TPU v7x, 256 devices: a whole 4x4x8 slice. The times are simulated.
256 devices in a mesh: leaf: 2 (over core), row: 8 (over z), col: 16 (over y, x).
Axes of the slice: x: 4, y: 4, z: 8, core: 2. Of those that a mesh axis runs over, the one named last changes fastest.
Arguments:
- front: float32 [2, 8, 8, 128, 4, 16, 128], P('leaf', None, 'row', None, None, 'col'), as said below
- parent: float32 [4, 2, 8, 128, 4, 16, 128], P(None, 'leaf', 'row', None, None, 'col'), may hold values from -0.2 to 0.2
- tile_map: int32 [2, 56], replicated, may hold values from 0 to 63, as said below
- col_shift: int32 [4], replicated, may hold values from 0 to 7
Outputs:
- factored: float32 [2, 8, 8, 128, 4, 16, 128], P('leaf', None, 'row', None, None, 'col')
- new_parent: float32 [4, 2, 8, 128, 4, 16, 128], P(None, 'leaf', 'row', None, None, 'col')
Inputs may be any that keep to these rules, and one draw needn't show every extreme that they name: For each leaf the 8192 x 8192 matrix read from front is symmetric positive definite. Entry [l, e] names the parent tile joined by tile 8 + e of child l; no row repeats a value. The parent tile q = tile_map[l, e] has (q mod 16 + col_shift[q // 16]) mod 16 equal to (8 + e) mod 16. Among the tiles of one child whose indices are equal mod 8, at most 1 have parent tiles equal mod 16.
All inputs are finite; a program needn't handle non-finite values.
Results may differ from a plain program's by a relative error of at most 0.0001.
Values sent between devices are 32-bit elements; how exact they have to be, the bound alone decides.
No kernel may reach another device: no remote copies, remote signals or barrier semaphores. Data moves between devices by JAX's collectives and lax.ppermute only.
A program may use at most 128 MiB of HBM per device.

v0:
```python
import jax
import jax.numpy as jnp
from jax import lax
from jax.sharding import PartitionSpec as P

TILE = 128
PB = 512
PANELS = 2
NPIV = 1024
HIGHEST = lax.Precision.HIGHEST


def spread(value, axis, source):
    kept = jnp.where(lax.axis_index(axis) == source, value, 0).astype(value.dtype)
    return lax.psum(kept, axis)


def update_slots(working, next_rows, column_factor, slot_low, slot_high):
    product = jnp.einsum(
        "atp,bsp->atbs",
        next_rows,
        column_factor,
        precision=HIGHEST,
        preferred_element_type=jnp.float32,
    )
    return working.at[:, :, slot_low:slot_high, :].add(-product)


def tall_cholesky(diagonal_block, below_rows):
    size = diagonal_block.shape[0]
    remaining = diagonal_block
    eye = jnp.eye(TILE, dtype=jnp.float32)
    diag_columns = []
    inverses = []
    for step in range(size // TILE):
        low = step * TILE
        left = size - low - TILE
        pivot = remaining[:TILE, :TILE]
        pivot_factor = jnp.linalg.cholesky(pivot)
        pivot_inverse = lax.linalg.triangular_solve(pivot_factor, eye, left_side=True, lower=True)
        inverses.append(pivot_inverse)
        parts = [jnp.zeros((low, TILE), jnp.float32), pivot_factor]
        if left:
            solved = jnp.dot(
                remaining[TILE:, :TILE],
                pivot_inverse.T,
                precision=HIGHEST,
                preferred_element_type=jnp.float32,
            )
            parts.append(solved)
            update = jnp.dot(
                solved, solved.T, precision=HIGHEST, preferred_element_type=jnp.float32
            )
            remaining = remaining[TILE:, TILE:] - update
        diag_columns.append(jnp.concatenate(parts, axis=0))
    lower_factor = jnp.concatenate(diag_columns, axis=1)
    rest = below_rows
    below_columns = []
    for step in range(size // TILE):
        low = step * TILE
        solved = jnp.dot(
            rest[:, :TILE], inverses[step].T, precision=HIGHEST, preferred_element_type=jnp.float32
        )
        below_columns.append(solved)
        if low + TILE < size:
            update = jnp.dot(
                solved,
                lower_factor[low + TILE :, low : low + TILE].T,
                precision=HIGHEST,
                preferred_element_type=jnp.float32,
            )
            rest = rest[:, TILE:] - update
    return (lower_factor, jnp.concatenate(below_columns, axis=1))


def per_device(front, parent, tile_map, col_shift):
    leaf_count = lax.axis_size("leaf")
    row_count = lax.axis_size("row")
    col_count = lax.axis_size("col")
    leaf_index = lax.axis_index("leaf")
    row_index = lax.axis_index("row")
    col_index = lax.axis_index("col")
    local_front = front[0, :, 0, :, :, 0, :]
    row_slots = local_front.shape[0]
    col_slots = local_front.shape[2]
    pivot_tiles = NPIV // TILE
    assert pivot_tiles == row_count and pivot_tiles <= col_count
    row_tiles = jnp.arange(row_slots, dtype=jnp.int32) * row_count + row_index
    col_tiles = jnp.arange(col_slots, dtype=jnp.int32) * col_count + col_index
    working = local_front
    first_tiles = lax.all_gather(working[0, :, 0, :], "col", axis=0, tiled=False)
    diag_row = first_tiles[:pivot_tiles].transpose(1, 0, 2).reshape(TILE, NPIV)
    diagonal_block = lax.all_gather(diag_row, "row", axis=0, tiled=True)
    rest_cols, top_input, diagonal_block = lax.optimization_barrier(
        (working[1:, :, 0, :], working[0], diagonal_block)
    )
    first_cols = lax.all_gather(rest_cols, "col", axis=0, tiled=False)
    row_panel = first_cols[:pivot_tiles].transpose(1, 2, 0, 3).reshape(row_slots - 1, TILE, NPIV)
    top_rows = lax.all_gather(top_input, "row", axis=0, tiled=False)
    column_panel = top_rows.transpose(2, 3, 0, 1).reshape(col_slots, TILE, NPIV)
    stacked = jnp.concatenate([row_panel.reshape(-1, NPIV), column_panel.reshape(-1, NPIV)], axis=0)
    lower_factor, solved = tall_cholesky(diagonal_block, stacked)
    trailing_rows = (row_slots - 1) * TILE
    row_factor = solved[:trailing_rows].reshape(row_slots - 1, TILE, NPIV)
    column_factor = solved[trailing_rows:].reshape(col_slots, TILE, NPIV)
    column_factor = jnp.where((col_tiles >= pivot_tiles)[:, None, None], column_factor, 0.0)
    product = jnp.einsum(
        "atk,bsk->atbs",
        row_factor,
        column_factor,
        precision=HIGHEST,
        preferred_element_type=jnp.float32,
    )
    trailing = working[1:] - product
    own_col = jnp.minimum(col_index, pivot_tiles - 1)
    row_factor_cols = lax.dynamic_slice_in_dim(row_factor, own_col * TILE, TILE, 2)
    is_factor_col = (col_tiles < pivot_tiles)[None, None, :, None]
    trailing = jnp.where(is_factor_col, row_factor_cols[:, :, None, :], trailing)
    diag_rows = lax.dynamic_slice_in_dim(lower_factor, row_index * TILE, TILE, 0)
    diag_tile = lax.dynamic_slice_in_dim(diag_rows, own_col * TILE, TILE, 1)
    local_ids = jnp.arange(TILE, dtype=jnp.int32)
    global_row = row_index * TILE + local_ids[:, None]
    global_col = own_col * TILE + local_ids[None, :]
    diag_tile = jnp.where(global_row >= global_col, diag_tile, 0.0)
    top = jnp.where(is_factor_col[0], diag_tile[:, None, :], 0.0)
    top = jnp.broadcast_to(top, working[0].shape)
    working = jnp.concatenate([top[None], trailing], axis=0)
    factored = working.reshape(front.shape)
    contribution = jnp.where((col_tiles >= pivot_tiles)[None, None, :, None], working, 0.0)
    contrib_count = tile_map.shape[1]
    entry_ids = jnp.arange(contrib_count, dtype=jnp.int32)
    own_map = lax.dynamic_index_in_dim(tile_map, leaf_index, 0, keepdims=False)
    row_match = (row_tiles - pivot_tiles)[:, None] == entry_ids[None, :]
    row_targets = jnp.sum(jnp.where(row_match, own_map[None, :], 0), axis=1)
    row_valid = row_tiles >= pivot_tiles
    owner_count = leaf_count * row_count
    destination = row_targets % owner_count
    parent_row_slot = row_targets // owner_count
    slot_ids = jnp.arange(row_slots, dtype=jnp.int32)
    same_before = (
        (destination[None, :] == destination[:, None])
        & row_valid[None, :]
        & (slot_ids[None, :] < slot_ids[:, None])
    )
    rank_in_dest = jnp.sum(same_before.astype(jnp.int32), axis=1)
    capacity = (col_slots + row_count - 1) // row_count
    owner_ids = jnp.arange(owner_count, dtype=jnp.int32)
    capacity_ids = jnp.arange(capacity, dtype=jnp.int32)
    selection = (
        row_valid[None, None, :]
        & (destination[None, None, :] == owner_ids[:, None, None])
        & (rank_in_dest[None, None, :] == capacity_ids[None, :, None])
    )
    flattened = contribution.reshape(row_slots, -1)
    send_buffer = jnp.einsum(
        "oka,ax->okx",
        selection.astype(jnp.float32),
        flattened,
        precision=HIGHEST,
        preferred_element_type=jnp.float32,
    )
    chosen_slot = jnp.sum(jnp.where(selection, parent_row_slot[None, None, :], 0), axis=2)
    send_slots = jnp.where(jnp.any(selection, axis=2), chosen_slot, -1)
    received, received_slots = (
        lax.all_to_all(send_buffer, ("leaf", "row"), split_axis=0, concat_axis=0, tiled=True),
        lax.all_to_all(send_slots, ("leaf", "row"), split_axis=0, concat_axis=0, tiled=True),
    )
    received = received.reshape(leaf_count, row_count, capacity, -1)
    received_slots = received_slots.reshape(leaf_count, row_count, capacity)
    parent_local = parent[:, 0, 0, :, :, 0, :]
    parent_rows = parent_local.shape[0]
    parent_cols = parent_local.shape[2]
    row_place = (
        received_slots[None] == jnp.arange(parent_rows, dtype=jnp.int32)[:, None, None, None]
    ).astype(jnp.float32)
    by_leaf = jnp.einsum(
        "slrk,lrkx->slx", row_place, received, precision=HIGHEST, preferred_element_type=jnp.float32
    )
    by_leaf = by_leaf.reshape(parent_rows, leaf_count, TILE, col_slots, TILE)
    col_match = (col_tiles - pivot_tiles)[:, None] == entry_ids[None, :]
    col_targets = jnp.sum(jnp.where(col_match[None], tile_map[:, None, :], 0), axis=2)
    col_valid = col_tiles >= pivot_tiles
    parent_slot_ids = jnp.arange(parent_cols, dtype=jnp.int32)
    col_place = (
        col_valid[None, None, :]
        & (col_targets[:, None, :] // col_count == parent_slot_ids[None, :, None])
    ).astype(jnp.float32)
    assembled = jnp.einsum(
        "sltbv,lub->stuv", by_leaf, col_place, precision=HIGHEST, preferred_element_type=jnp.float32
    )
    new_parent = (parent_local + assembled).reshape(parent.shape)
    return (factored, new_parent)


def solution(mesh):
    return jax.shard_map(
        per_device,
        mesh=mesh,
        in_specs=(
            P("leaf", None, "row", None, None, "col", None),
            P(None, "leaf", "row", None, None, "col", None),
            P(),
            P(),
        ),
        out_specs=(
            P("leaf", None, "row", None, None, "col", None),
            P(None, "leaf", "row", None, None, "col", None),
        ),
        check_vma=False,
    )
```

profile of v0, /device:TPU:1, one launch (start us, length us, event | category | flops | bytes accessed | tf_op | source)
XLA Modules:
  0.0 557.9 jit_solution(11037079520208860323)
XLA Ops:
  9.9 51.3 %all-gather.10.cloned.1.call-done = f32[16,128,1,128]{3,1,2,0:T(8,128)} async-done(((f32[1,128,1,128]{3,1,2,0:T(8,128)}), f32[16,128,1,128]{3,1,2,0:T(8,128)}) %all-gather.10.cloned.1.call-update) | async-done | bytes 1048592 | tf_op jit(solution)/shard_map/all_gather | solution.py:91
  65.8 58.1 %all-gather.8.cloned.1.call-done = f32[1024,1024]{0,1:T(8,128)} async-done(((f32[128,1024]{0,1:T(8,128)}), f32[1024,1024]{0,1:T(8,128)}) %all-gather.8.cloned.1.call-update) | async-done | bytes 4194320 | tf_op jit(solution)/shard_map/all_gather | solution.py:93
  125.8 8.8 %all-to-all-start.1 = ((s32[16,1,1]{2,1,0:T(1,128)}), s32[16,1,1]{2,1,0:T(1,128)S(1)}, u32[]{:S(2)}, u32[]{:S(2)}) async-start(s32[16,1,1]{2,1,0:T(1,128)} %copy.138), calls=%async_computation.1 | async-start | bytes 16384 | tf_op jit(solution)/shard_map/all_to_all | solution.py:166
  139.9 11.7 %cholesky.134 = f32[128,128]{1,0:T(8,128)S(1)} custom-call(f32[128,128]{1,0:T(8,128)S(1)} %fusion.68), custom_call_target="Cholesky" | custom-call | tf_op jit(solution)/shard_map/jit(cholesky)/cholesky | solution.py:39
  153.6 9.8 %custom-call.12 = f32[1,128,128]{1,2,0:T(8,128)S(1)} custom-call(f32[1,128,128]{2,1,0:T(8,128)S(1)} %get-tuple-element.34), custom_call_target="InvertDiagBlocksLowerTriangular" | custom-call | tf_op jit(solution)/shard_map/triangular_solve/custom-call.0 | solution.py:40
  167.0 4.6 slice_subtract_fusion.2
  171.7 12.0 %cholesky.145 = f32[128,128]{1,0:T(8,128)S(1)} custom-call(f32[128,128]{1,0:T(8,128)S(1)} %fusion.66), custom_call_target="Cholesky" | custom-call | tf_op jit(solution)/shard_map/jit(cholesky)/cholesky | solution.py:39
  185.7 9.8 %custom-call.13 = f32[1,128,128]{1,2,0:T(8,128)S(1)} custom-call(f32[1,128,128]{2,1,0:T(8,128)S(1)} %get-tuple-element.32), custom_call_target="InvertDiagBlocksLowerTriangular" | custom-call | tf_op jit(solution)/shard_map/triangular_solve/custom-call.0 | solution.py:40
  201.7 11.7 %cholesky.156 = f32[128,128]{1,0:T(8,128)S(1)} custom-call(f32[128,128]{1,0:T(8,128)S(1)} %fusion.64), custom_call_target="Cholesky" | custom-call | tf_op jit(solution)/shard_map/jit(cholesky)/cholesky | solution.py:39
  215.4 10.0 %custom-call.14 = f32[1,128,128]{1,2,0:T(8,128)S(1)} custom-call(f32[1,128,128]{2,1,0:T(8,128)S(1)} %get-tuple-element.30), custom_call_target="InvertDiagBlocksLowerTriangular" | custom-call | tf_op jit(solution)/shard_map/triangular_solve/custom-call.0 | solution.py:40
  231.0 11.7 %cholesky.167 = f32[128,128]{1,0:T(8,128)S(1)} custom-call(f32[128,128]{1,0:T(8,128)S(1)} %fusion.62), custom_call_target="Cholesky" | custom-call | tf_op jit(solution)/shard_map/jit(cholesky)/cholesky | solution.py:39
  244.7 9.8 %custom-call.15 = f32[1,128,128]{1,2,0:T(8,128)S(1)} custom-call(f32[1,128,128]{2,1,0:T(8,128)S(1)} %get-tuple-element.28), custom_call_target="InvertDiagBlocksLowerTriangular" | custom-call | tf_op jit(solution)/shard_map/triangular_solve/custom-call.0 | solution.py:40
  257.2 11.9 %cholesky.178 = f32[128,128]{1,0:T(8,128)S(1)} custom-call(f32[128,128]{1,0:T(8,128)S(1)} %fusion.60), custom_call_target="Cholesky" | custom-call | tf_op jit(solution)/shard_map/jit(cholesky)/cholesky | solution.py:39
  271.1 9.8 %custom-call.16 = f32[1,128,128]{1,2,0:T(8,128)S(1)} custom-call(f32[1,128,128]{2,1,0:T(8,128)S(1)} %get-tuple-element.26), custom_call_target="InvertDiagBlocksLowerTriangular" | custom-call | tf_op jit(solution)/shard_map/triangular_solve/custom-call.0 | solution.py:40
  282.5 11.7 %cholesky.189 = f32[128,128]{1,0:T(8,128)S(1)} custom-call(f32[128,128]{1,0:T(8,128)S(1)} %fusion.58), custom_call_target="Cholesky" | custom-call | tf_op jit(solution)/shard_map/jit(cholesky)/cholesky | solution.py:39
  295.6 9.8 %custom-call.17 = f32[1,128,128]{1,2,0:T(8,128)S(1)} custom-call(f32[1,128,128]{2,1,0:T(8,128)S(1)} %get-tuple-element.24), custom_call_target="InvertDiagBlocksLowerTriangular" | custom-call | tf_op jit(solution)/shard_map/triangular_solve/custom-call.0 | solution.py:40
  309.0 11.7 %cholesky.200 = f32[128,128]{1,0:T(8,128)S(1)} custom-call(f32[128,128]{1,0:T(8,128)S(1)} %fusion.56), custom_call_target="Cholesky" | custom-call | tf_op jit(solution)/shard_map/jit(cholesky)/cholesky | solution.py:39
  322.1 9.8 %custom-call.18 = f32[1,128,128]{1,2,0:T(8,128)S(1)} custom-call(f32[1,128,128]{2,1,0:T(8,128)S(1)} %get-tuple-element.22), custom_call_target="InvertDiagBlocksLowerTriangular" | custom-call | tf_op jit(solution)/shard_map/triangular_solve/custom-call.0 | solution.py:40
  332.9 11.7 %cholesky.211 = f32[128,128]{1,0:T(8,128)S(1)} custom-call(f32[128,128]{1,0:T(8,128)S(1)} %fusion.54), custom_call_target="Cholesky" | custom-call | tf_op jit(solution)/shard_map/jit(cholesky)/cholesky | solution.py:39
  345.9 10.0 %custom-call.19 = f32[1,128,128]{1,2,0:T(8,128)S(1)} custom-call(f32[1,128,128]{2,1,0:T(8,128)S(1)} %get-tuple-element.20), custom_call_target="InvertDiagBlocksLowerTriangular" | custom-call | tf_op jit(solution)/shard_map/triangular_solve/custom-call.0 | solution.py:40
  369.8 5.4 slice_subtract_fusion
  376.1 3.8 slice_subtract_fusion.1
  380.7 3.9 convolution_subtract_fusion
  401.8 5.1 copy.133
  411.6 8.9 %fusion.5 = f32[7,128,4,128]{3,1,2,0:T(8,128)S(1)} fusion(f32[1,8,1,128,4,1,128]{6,3,4,1,5,2,0:T(8,128)} %copy-done.4, f32[7,128,1024,1]{2,1,3,0:T(8,128)} %bitcast.198, f32[4,128,1024,1]{2,1,0,3:T(8,128)} %bitcast.203, f32[7,128,128]{2,1,0:T(8,128)S(1)} %constant_dynamic-slice_fusion, pred[4]{0:T(512)(128)(4,1)S(1)} %copy-done.44), kind=kOutput, calls=%fused_computation.23 | convolution fusion | flops 5638062080 | bytes 9895940 | tf_op jit(solution)/shard_map/atk,bsk->atbs/dot_general | solution.py:107
  423.0 3.7 concatenate.53
  426.8 3.8 convolution_bitcast_fusion
  430.6 6.3 %copy.137 = f32[16,1,65536]{2,1,0:T(1,128)} copy(f32[16,1,65536]{2,0,1:T(8,128)S(1)} %convolution_bitcast_fusion) | data formatting | bytes 8388608 | tf_op jit(solution)/shard_map/oka,ax->okx/dot_general | solution.py:155
  436.9 7.6 %all-to-all-start = ((f32[16,1,65536]{2,1,0:T(1,128)}), f32[16,1,65536]{2,1,0:T(1,128)}, u32[]{:S(2)}, u32[]{:S(2)}) async-start(f32[16,1,65536]{2,1,0:T(1,128)} %copy.137), calls=%async_computation | async-start | bytes 8388608 | tf_op jit(solution)/shard_map/all_to_all | solution.py:165
  445.6 3.5 copy.140
  449.1 88.1 %all-to-all-done = f32[16,1,65536]{2,1,0:T(1,128)} async-done(((f32[16,1,65536]{2,1,0:T(1,128)}), f32[16,1,65536]{2,1,0:T(1,128)}, u32[]{:S(2)}, u32[]{:S(2)}) %all-to-all-start) | async-done | bytes 4194336 | tf_op jit(solution)/shard_map/all_to_all | solution.py:165
  537.2 7.8 %convolution_bitcast_fusion.1 = f32[4,2,65536]{2,0,1:T(4,128)} fusion(f32[16,1,65536]{2,1,0:T(1,128)} %all-to-all-done, s32[2,8]{1,0:T(2,128)S(1)} %eq.153), kind=kOutput, calls=%fused_computation.1 | convolution fusion | flops 50331712 | bytes 6291520 | tf_op jit(solution)/shard_map/slrk,lrkx->slx/dot_general | solution.py:176
  (262 shorter events, 98.8 us)
Async XLA Ops:
  7.2 116.8 %copy-start.51 = (s32[2,56]{1,0:T(2,128)S(1)}, s32[2,56]{1,0:T(2,128)}, u32[]{:S(2)}) copy-start(s32[2,56]{1,0:T(2,128)} %param.9) | copy-start | bytes 1348
  7.2 54.0 %all-gather.10.cloned.1.call-start = ((), (), s32[]{:S(2)}) async-start(), calls=%async_computation.3 | async-start | bytes 1114112 | tf_op jit(solution)/shard_map/all_gather | solution.py:91
  9.1 154.6 %copy-start.4 = (f32[1,8,1,128,4,1,128]{6,3,4,1,5,2,0:T(8,128)}, f32[1,8,1,128,4,1,128]{6,3,4,1,5,2,0:T(8,128)S(1)}, u32[]{:S(2)}) copy-start(f32[1,8,1,128,4,1,128]{6,3,4,1,5,2,0:T(8,128)S(1)} %copy.164) | copy-start | bytes 6291460
  9.8 114.1 %all-gather.8.cloned.1.call-start = ((), (), s32[]{:S(2)}) async-start(), calls=%async_computation.2 | async-start | bytes 4718592 | tf_op jit(solution)/shard_map/all_gather | solution.py:93
  63.2 297.6 %all-gather.14.cloned.1.call-start = ((), (), s32[]{:S(2)}) async-start(), calls=%async_computation.5 | async-start | bytes 2359296 | tf_op jit(solution)/shard_map/all_gather | solution.py:99
  123.9 239.2 %all-gather.12.cloned.1.call-start = ((), (), s32[]{:S(2)}) async-start(), calls=%async_computation.4 | async-start | bytes 7798784 | tf_op jit(solution)/shard_map/all_gather | solution.py:97
  125.8 311.2 %all-to-all-start.1 = ((s32[16,1,1]{2,1,0:T(1,128)}), s32[16,1,1]{2,1,0:T(1,128)S(1)}, u32[]{:S(2)}, u32[]{:S(2)}) async-start(s32[16,1,1]{2,1,0:T(1,128)} %copy.138), calls=%async_computation.1 | async-start | bytes 16384 | tf_op jit(solution)/shard_map/all_to_all | solution.py:166
  257.0 98.9 %copy-start.1 = (f32[896,128]{1,0:T(8,128)S(1)}, f32[896,128]{1,0:T(8,128)}, u32[]{:S(2)}) copy-start(f32[896,128]{1,0:T(8,128)} %copy-done) | copy-start | bytes 1376260
  269.8 87.1 %copy-start.3 = (f32[768,128]{1,0:T(8,128)S(1)}, f32[768,128]{1,0:T(8,128)}, u32[]{:S(2)}) copy-start(f32[768,128]{1,0:T(8,128)} %copy-done.2) | copy-start | bytes 1179652
  281.2 76.5 %copy-start.18 = (f32[128,128]{1,0:T(8,128)}, f32[128,128]{1,0:T(8,128)S(1)}, u32[]{:S(2)}) copy-start(f32[128,128]{1,0:T(8,128)S(1)} %fusion.37) | copy-start | bytes 196612
  281.7 76.5 %copy-start.7 = (f32[384,128]{1,0:T(8,128)}, f32[384,128]{1,0:T(8,128)S(1)}, u32[]{:S(2)}) copy-start(f32[384,128]{1,0:T(8,128)S(1)} %fusion.47) | copy-start | bytes 589828
  282.4 23.1 %copy-start.11 = (f32[384,384]{0,1:T(8,128)}, f32[384,384]{0,1:T(8,128)S(1)}, u32[]{:S(2)}) copy-start(f32[384,384]{0,1:T(8,128)S(1)} %convolution_subtract_fusion.6) | copy-start | bytes 1769476
  282.4 75.4 %copy-start.32 = (f32[128,128]{1,0:T(8,128)S(1)}, f32[128,128]{1,0:T(8,128)}, u32[]{:S(2)}) copy-start(f32[128,128]{1,0:T(8,128)} %get-tuple-element.31) | copy-start | bytes 196612
  282.4 75.4 %copy-start.36 = (f32[1024]{0:T(1024)S(1)}, f32[1024]{0:T(1024)}, u32[]{:S(2)}) copy-start(f32[1024]{0:T(1024)} %pad.10.clone) | copy-start | bytes 12292
  282.4 75.6 %copy-start.35 = (f32[128,128]{1,0:T(8,128)S(1)}, f32[128,128]{1,0:T(8,128)}, u32[]{:S(2)}) copy-start(f32[128,128]{1,0:T(8,128)} %get-tuple-element.29) | copy-start | bytes 196612
  282.4 75.6 %copy-start.38 = (f32[1024]{0:T(1024)S(1)}, f32[1024]{0:T(1024)}, u32[]{:S(2)}) copy-start(f32[1024]{0:T(1024)} %pad.13.clone) | copy-start | bytes 12292
  294.3 63.9 %copy-start.33 = (f32[128,128]{1,0:T(8,128)S(1)}, f32[128,128]{1,0:T(8,128)}, u32[]{:S(2)}) copy-start(f32[128,128]{1,0:T(8,128)} %get-tuple-element.27) | copy-start | bytes 196612
  294.3 63.9 %copy-start.37 = (f32[1024]{0:T(1024)S(1)}, f32[1024]{0:T(1024)}, u32[]{:S(2)}) copy-start(f32[1024]{0:T(1024)} %pad.16.clone) | copy-start | bytes 12292
  306.1 52.3 %copy-start.20 = (f32[128,128]{1,0:T(8,128)}, f32[128,128]{1,0:T(8,128)S(1)}, u32[]{:S(2)}) copy-start(f32[128,128]{1,0:T(8,128)S(1)} %fusion.35) | copy-start | bytes 196612
  307.5 51.0 %copy-start.9 = (f32[256,128]{1,0:T(8,128)}, f32[256,128]{1,0:T(8,128)S(1)}, u32[]{:S(2)}) copy-start(f32[256,128]{1,0:T(8,128)S(1)} %fusion.49) | copy-start | bytes 393220
  332.2 26.8 %copy-start.24 = (f32[128,128]{1,0:T(8,128)}, f32[128,128]{1,0:T(8,128)S(1)}, u32[]{:S(2)}) copy-start(f32[128,128]{1,0:T(8,128)S(1)} %fusion.33) | copy-start | bytes 196612
  332.5 26.5 %copy-start.12 = (f32[128,128]{1,0:T(8,128)}, f32[128,128]{1,0:T(8,128)S(1)}, u32[]{:S(2)}) copy-start(f32[128,128]{1,0:T(8,128)S(1)} %fusion.51) | copy-start | bytes 196612
  332.7 26.2 %copy-start.49 = (s32[128]{0:T(128)S(1)}, s32[128]{0:T(128)}, u32[]{:S(2)}) copy-start(s32[128]{0:T(128)} %get-tuple-element.56) | copy-start | bytes 1540
  332.8 26.2 %copy-start.50 = (s32[128]{0:T(128)S(1)}, s32[128]{0:T(128)}, u32[]{:S(2)}) copy-start(s32[128]{0:T(128)} %get-tuple-element.57) | copy-start | bytes 1540
  332.9 27.1 %copy-start.43 = (pred[4]{0:T(512)(128)(4,1)S(1)}, pred[4]{0:T(512)(128)(4,1)}, u32[]{:S(2)}) copy-start(pred[4]{0:T(512)(128)(4,1)} %get-tuple-element.55) | copy-start | bytes 16
  420.5 6.3 %copy-start.15 = (f32[128,4,128]{2,1,0:T(4,128)S(1)}, f32[128,4,128]{2,1,0:T(4,128)}, u32[]{:S(2)}) copy-start(f32[128,4,128]{2,1,0:T(4,128)} %broadcast_select_fusion) | copy-start | bytes 786436
  420.5 6.3 %copy-start.40 = (s32[8]{0:T(128)S(1)}, s32[8]{0:T(128)}, u32[]{:S(2)}) copy-start(s32[8]{0:T(128)} %copy-done.39) | copy-start | bytes 100
  420.5 6.3 %copy-start.42 = (pred[8]{0:T(512)(128)(4,1)S(1)}, pred[8]{0:T(512)(128)(4,1)}, u32[]{:S(2)}) copy-start(pred[8]{0:T(512)(128)(4,1)} %copy-done.41) | copy-start | bytes 28
  420.6 6.3 %copy-start.46 = (pred[8]{0:T(512)(128)(4,1)S(1)}, pred[8]{0:T(512)(128)(4,1)}, u32[]{:S(2)}) copy-start(pred[8]{0:T(512)(128)(4,1)} %copy-done.45) | copy-start | bytes 28
  436.9 7.7 %copy-start.52 = (s32[2,56]{1,0:T(2,128)S(1)}, s32[2,56]{1,0:T(2,128)}, u32[]{:S(2)}) copy-start(s32[2,56]{1,0:T(2,128)} %param.9) | copy-start | bytes 1348
  436.9 8.4 %copy-start.23 = (f32[128,128]{1,0:T(8,128)S(1)}, f32[128,128]{1,0:T(8,128)}, u32[]{:S(2)}) copy-start(f32[128,128]{1,0:T(8,128)} %copy-done.22) | copy-start | bytes 196612
  436.9 100.2 %all-to-all-start = ((f32[16,1,65536]{2,1,0:T(1,128)}), f32[16,1,65536]{2,1,0:T(1,128)}, u32[]{:S(2)}, u32[]{:S(2)}) async-start(f32[16,1,65536]{2,1,0:T(1,128)} %copy.137), calls=%async_computation | async-start | bytes 8388608 | tf_op jit(solution)/shard_map/all_to_all | solution.py:165
  (29 other events, 71.0 us)
Sparse Core Ops, SparseCore 0:
  11.0 50.0 all-gather.9
  63.4 60.4 all-gather.7
  125.7 38.9 all-gather.13
  167.0 73.5 all-gather.11
where the time goes:
time: 568 us; the launch traced here: 558 us
  waiting for transfers between devices  198 us (35%)
  other arithmetic  197 us (35%)
  matrix products  74.3 us (13%)
  local copies, waits for them, and re-layouts  57.1 us (10%)
  starting transfers between devices  16.6 us (3%)
  between operations  15.6 us (3%)
    another operation x24, other arithmetic, tall_cholesky(): pivot_factor = jnp.linalg.cholesky(pivot)  99.6 us
    all_to_all x1, waiting for transfers between devices, per_device(): lax.all_to_all(send_buffer, ('leaf', 'row'), split_axis=0, concat_axis=0,...  88.1 us
    another operation x16, other arithmetic, tall_cholesky(): lax.linalg.triangular_solve(pivot_factor, eye, left_side=True, lower=True)  87.2 us
    all_gather x1, waiting for transfers between devices, per_device(): diagonal_block = lax.all_gather(diag_row, 'row', axis=0, tiled=True)  58.1 us
    all_gather x1, waiting for transfers between devices, per_device(): lax.all_gather(working[0, :, 0, :], 'col', axis=0, tiled=False)  51.3 us
    dot_general x7, matrix products, tall_cholesky(): jnp.dot(solved, lower_factor[low + TILE:, low:low + TILE].T, precision=HI...  21.2 us
    unnamed x111, local copies, waits for them, and re-layouts  14.3 us
    dot_general x7, matrix products, tall_cholesky(): jnp.dot(solved, solved.T, precision=HIGHEST, preferred_element_type=jnp.f...  12.8 us
  transfers between devices with their start and end apart: 6, of which 3 were waited for; matrix products, arithmetic and copies ran while one was open for 54% of the time, Pallas kernels for 0%

commit v1 on v0

--- a/solution.py
+++ b/solution.py
@@ -90,7 +90,10 @@
     working = local_front
     first_tiles = lax.all_gather(working[0, :, 0, :], "col", axis=0, tiled=False)
     diag_row = first_tiles[:pivot_tiles].transpose(1, 0, 2).reshape(TILE, NPIV)
-    diagonal_block = lax.all_gather(diag_row, "row", axis=0, tiled=True)
+    count = lax.axis_size("row")
+    blocks = jnp.stack([diag_row for _ in range(count)])
+    blocks = lax.all_to_all(blocks, "row", split_axis=0, concat_axis=0)
+    diagonal_block = jnp.concatenate(blocks, axis=0)
     rest_cols, top_input, diagonal_block = lax.optimization_barrier(
         (working[1:, :, 0, :], working[0], diagonal_block)
     )

time: 568 us -> 613 us (1.079)
  waiting for transfers between devices: 198 us -> 234 us
  local copies, waits for them, and re-layouts: 57.1 us -> 63.4 us
    all_to_all x0 -> x1, waiting for transfers between devices: none -> 94.3 us  [per_device(): blocks = lax.all_to_all(blocks, 'row', split_axis=0, concat_axis=0)]
    all_gather x1 -> x0, waiting for transfers between devices: 58.1 us -> none  [per_device(): diagonal_block = lax.all_gather(diag_row, 'row', axis=0, tiled=True)]
    all_to_all x0 -> x1, starting transfers between devices: none -> 6.73 us  [per_device(): blocks = lax.all_to_all(blocks, 'row', split_axis=0, concat_axis=0)]
    unnamed x111 -> x112, local copies, waits for them, and re-layouts: 14.3 us -> 14.6 us
  transfers between devices with their start and end apart: 6 -> 6, of which waited for: 3 -> 3; matrix products, arithmetic and copies ran while one was open for 54% -> 50% of each run, Pallas kernels for 0% -> 0%
where the time goes in v1:
time: 613 us; the launch traced here: 602 us
  waiting for transfers between devices  234 us (38%)
  other arithmetic  197 us (32%)
  matrix products  74.3 us (12%)
  local copies, waits for them, and re-layouts  63.4 us (10%)
  starting transfers between devices  18.2 us (3%)
  between operations  15.6 us (3%)
    another operation x24, other arithmetic, tall_cholesky(): pivot_factor = jnp.linalg.cholesky(pivot)  99.6 us
    all_to_all x1, waiting for transfers between devices, per_device(): blocks = lax.all_to_all(blocks, 'row', split_axis=0, concat_axis=0)  94.3 us
    all_to_all x1, waiting for transfers between devices, per_device(): lax.all_to_all(send_buffer, ('leaf', 'row'), split_axis=0, concat_axis=0,...  88.1 us
    another operation x16, other arithmetic, tall_cholesky(): lax.linalg.triangular_solve(pivot_factor, eye, left_side=True, lower=True)  87 us
    all_gather x1, waiting for transfers between devices, per_device(): lax.all_gather(working[0, :, 0, :], 'col', axis=0, tiled=False)  51.3 us
    dot_general x7, matrix products, tall_cholesky(): jnp.dot(solved, lower_factor[low + TILE:, low:low + TILE].T, precision=HI...  21.2 us
    unnamed x112, local copies, waits for them, and re-layouts  14.6 us
    dot_general x7, matrix products, tall_cholesky(): jnp.dot(solved, solved.T, precision=HIGHEST, preferred_element_type=jnp.f...  12.8 us
  transfers between devices with their start and end apart: 6, of which 3 were waited for; matrix products, arithmetic and copies ran while one was open for 50% of the time, Pallas kernels for 0%

profile of v1, /device:TPU:1, one launch (start us, length us, event | category | flops | bytes accessed | tf_op | source)
XLA Modules:
  0.0 601.8 jit_solution(5237408563387931805)
XLA Ops:
  9.8 51.3 %all-gather.7.cloned.1.call-done = f32[16,128,1,128]{3,1,2,0:T(8,128)} async-done(((f32[1,128,1,128]{3,1,2,0:T(8,128)}), f32[16,128,1,128]{3,1,2,0:T(8,128)}) %all-gather.7.cloned.1.call-update) | async-done | bytes 1048592 | tf_op jit(solution)/shard_map/all_gather | solution.py:91
  64.7 6.7 %all-to-all-start = ((f32[8,128,1024]{1,2,0:T(8,128)}), f32[8,128,1024]{1,2,0:T(8,128)}, u32[]{:S(2)}, u32[]{:S(2)}) async-start(f32[8,128,1024]{1,2,0:T(8,128)} %stack.3), calls=%async_computation | async-start | bytes 8388608 | tf_op jit(solution)/shard_map/all_to_all | solution.py:95
  74.0 94.3 %all-to-all-done = f32[8,128,1024]{1,2,0:T(8,128)} async-done(((f32[8,128,1024]{1,2,0:T(8,128)}), f32[8,128,1024]{1,2,0:T(8,128)}, u32[]{:S(2)}, u32[]{:S(2)}) %all-to-all-start) | async-done | bytes 4194336 | tf_op jit(solution)/shard_map/all_to_all | solution.py:95
  168.3 4.8 copy_bitcast_fusion
  175.0 3.7 all-to-all-start.2
  184.1 11.7 %cholesky.134 = f32[128,128]{1,0:T(8,128)S(1)} custom-call(f32[128,128]{1,0:T(8,128)S(1)} %fusion.68), custom_call_target="Cholesky" | custom-call | tf_op jit(solution)/shard_map/jit(cholesky)/cholesky | solution.py:39
  197.7 9.8 %custom-call.12 = f32[1,128,128]{1,2,0:T(8,128)S(1)} custom-call(f32[1,128,128]{2,1,0:T(8,128)S(1)} %get-tuple-element.34), custom_call_target="InvertDiagBlocksLowerTriangular" | custom-call | tf_op jit(solution)/shard_map/triangular_solve/custom-call.0 | solution.py:40
  211.1 4.6 slice_subtract_fusion.2
  215.9 12.0 %cholesky.145 = f32[128,128]{1,0:T(8,128)S(1)} custom-call(f32[128,128]{1,0:T(8,128)S(1)} %fusion.66), custom_call_target="Cholesky" | custom-call | tf_op jit(solution)/shard_map/jit(cholesky)/cholesky | solution.py:39
  229.9 9.8 %custom-call.13 = f32[1,128,128]{1,2,0:T(8,128)S(1)} custom-call(f32[1,128,128]{2,1,0:T(8,128)S(1)} %get-tuple-element.32), custom_call_target="InvertDiagBlocksLowerTriangular" | custom-call | tf_op jit(solution)/shard_map/triangular_solve/custom-call.0 | solution.py:40
  245.9 11.7 %cholesky.156 = f32[128,128]{1,0:T(8,128)S(1)} custom-call(f32[128,128]{1,0:T(8,128)S(1)} %fusion.64), custom_call_target="Cholesky" | custom-call | tf_op jit(solution)/shard_map/jit(cholesky)/cholesky | solution.py:39
  259.5 10.0 %custom-call.14 = f32[1,128,128]{1,2,0:T(8,128)S(1)} custom-call(f32[1,128,128]{2,1,0:T(8,128)S(1)} %get-tuple-element.30), custom_call_target="InvertDiagBlocksLowerTriangular" | custom-call | tf_op jit(solution)/shard_map/triangular_solve/custom-call.0 | solution.py:40
  275.2 11.7 %cholesky.167 = f32[128,128]{1,0:T(8,128)S(1)} custom-call(f32[128,128]{1,0:T(8,128)S(1)} %fusion.62), custom_call_target="Cholesky" | custom-call | tf_op jit(solution)/shard_map/jit(cholesky)/cholesky | solution.py:39
  288.9 9.8 %custom-call.15 = f32[1,128,128]{1,2,0:T(8,128)S(1)} custom-call(f32[1,128,128]{2,1,0:T(8,128)S(1)} %get-tuple-element.28), custom_call_target="InvertDiagBlocksLowerTriangular" | custom-call | tf_op jit(solution)/shard_map/triangular_solve/custom-call.0 | solution.py:40
  301.3 11.9 %cholesky.178 = f32[128,128]{1,0:T(8,128)S(1)} custom-call(f32[128,128]{1,0:T(8,128)S(1)} %fusion.60), custom_call_target="Cholesky" | custom-call | tf_op jit(solution)/shard_map/jit(cholesky)/cholesky | solution.py:39
  315.2 9.8 %custom-call.16 = f32[1,128,128]{1,2,0:T(8,128)S(1)} custom-call(f32[1,128,128]{2,1,0:T(8,128)S(1)} %get-tuple-element.26), custom_call_target="InvertDiagBlocksLowerTriangular" | custom-call | tf_op jit(solution)/shard_map/triangular_solve/custom-call.0 | solution.py:40
  326.7 11.7 %cholesky.189 = f32[128,128]{1,0:T(8,128)S(1)} custom-call(f32[128,128]{1,0:T(8,128)S(1)} %fusion.58), custom_call_target="Cholesky" | custom-call | tf_op jit(solution)/shard_map/jit(cholesky)/cholesky | solution.py:39
  339.6 9.8 %custom-call.17 = f32[1,128,128]{1,2,0:T(8,128)S(1)} custom-call(f32[1,128,128]{2,1,0:T(8,128)S(1)} %get-tuple-element.24), custom_call_target="InvertDiagBlocksLowerTriangular" | custom-call | tf_op jit(solution)/shard_map/triangular_solve/custom-call.0 | solution.py:40
  353.0 11.7 %cholesky.200 = f32[128,128]{1,0:T(8,128)S(1)} custom-call(f32[128,128]{1,0:T(8,128)S(1)} %fusion.56), custom_call_target="Cholesky" | custom-call | tf_op jit(solution)/shard_map/jit(cholesky)/cholesky | solution.py:39
  366.0 9.8 %custom-call.18 = f32[1,128,128]{1,2,0:T(8,128)S(1)} custom-call(f32[1,128,128]{2,1,0:T(8,128)S(1)} %get-tuple-element.22), custom_call_target="InvertDiagBlocksLowerTriangular" | custom-call | tf_op jit(solution)/shard_map/triangular_solve/custom-call.0 | solution.py:40
  376.9 11.7 %cholesky.211 = f32[128,128]{1,0:T(8,128)S(1)} custom-call(f32[128,128]{1,0:T(8,128)S(1)} %fusion.54), custom_call_target="Cholesky" | custom-call | tf_op jit(solution)/shard_map/jit(cholesky)/cholesky | solution.py:39
  389.9 9.9 %custom-call.19 = f32[1,128,128]{1,2,0:T(8,128)S(1)} custom-call(f32[1,128,128]{2,1,0:T(8,128)S(1)} %get-tuple-element.20), custom_call_target="InvertDiagBlocksLowerTriangular" | custom-call | tf_op jit(solution)/shard_map/triangular_solve/custom-call.0 | solution.py:40
  413.8 5.4 slice_subtract_fusion
  420.0 3.8 slice_subtract_fusion.1
  424.6 3.9 convolution_subtract_fusion
  445.7 5.0 copy.135
  455.5 8.9 %fusion.5 = f32[7,128,4,128]{3,1,2,0:T(8,128)S(1)} fusion(f32[1,8,1,128,4,1,128]{6,3,4,1,5,2,0:T(8,128)} %copy-done.4, f32[7,128,1024,1]{2,1,3,0:T(8,128)} %bitcast.203, f32[4,128,1024,1]{2,1,0,3:T(8,128)} %bitcast.208, f32[7,128,128]{2,1,0:T(8,128)S(1)} %constant_dynamic-slice_fusion, pred[4]{0:T(512)(128)(4,1)S(1)} %copy-done.44), kind=kOutput, calls=%fused_computation.24 | convolution fusion | flops 5638062080 | bytes 9895940 | tf_op jit(solution)/shard_map/atk,bsk->atbs/dot_general | solution.py:110
  470.8 3.8 convolution_bitcast_fusion
  474.5 6.3 %copy.139 = f32[16,1,65536]{2,1,0:T(1,128)} copy(f32[16,1,65536]{2,0,1:T(8,128)S(1)} %convolution_bitcast_fusion) | data formatting | bytes 8388608 | tf_op jit(solution)/shard_map/oka,ax->okx/dot_general | solution.py:158
  480.9 7.6 %all-to-all-start.1 = ((f32[16,1,65536]{2,1,0:T(1,128)}), f32[16,1,65536]{2,1,0:T(1,128)}, u32[]{:S(2)}, u32[]{:S(2)}) async-start(f32[16,1,65536]{2,1,0:T(1,128)} %copy.139), calls=%async_computation.1 | async-start | bytes 8388608 | tf_op jit(solution)/shard_map/all_to_all | solution.py:168
  493.0 88.1 %all-to-all-done.1 = f32[16,1,65536]{2,1,0:T(1,128)} async-done(((f32[16,1,65536]{2,1,0:T(1,128)}), f32[16,1,65536]{2,1,0:T(1,128)}, u32[]{:S(2)}, u32[]{:S(2)}) %all-to-all-start.1) | async-done | bytes 4194336 | tf_op jit(solution)/shard_map/all_to_all | solution.py:168
  581.1 7.8 %convolution_bitcast_fusion.1 = f32[4,2,65536]{2,0,1:T(4,128)} fusion(f32[16,1,65536]{2,1,0:T(1,128)} %all-to-all-done.1, s32[2,8]{1,0:T(2,128)S(1)} %eq.153), kind=kOutput, calls=%fused_computation.1 | convolution fusion | flops 50331712 | bytes 6291520 | tf_op jit(solution)/shard_map/slrk,lrkx->slx/dot_general | solution.py:179
  (263 shorter events, 107.1 us)
Async XLA Ops:
  7.2 54.0 %all-gather.7.cloned.1.call-start = ((), (), s32[]{:S(2)}) async-start(), calls=%async_computation.3 | async-start | bytes 1114112 | tf_op jit(solution)/shard_map/all_gather | solution.py:91
  9.1 64.1 %copy-start.4 = (f32[1,8,1,128,4,1,128]{6,3,4,1,5,2,0:T(8,128)}, f32[1,8,1,128,4,1,128]{6,3,4,1,5,2,0:T(8,128)S(1)}, u32[]{:S(2)}) copy-start(f32[1,8,1,128,4,1,128]{6,3,4,1,5,2,0:T(8,128)S(1)} %copy.169) | copy-start | bytes 6291460
  64.7 103.6 %all-to-all-start = ((f32[8,128,1024]{1,2,0:T(8,128)}), f32[8,128,1024]{1,2,0:T(8,128)}, u32[]{:S(2)}, u32[]{:S(2)}) async-start(f32[8,128,1024]{1,2,0:T(8,128)} %stack.3), calls=%async_computation | async-start | bytes 8388608 | tf_op jit(solution)/shard_map/all_to_all | solution.py:95
  71.4 333.4 %all-gather.11.cloned.1.call-start = ((), (), s32[]{:S(2)}) async-start(), calls=%async_computation.5 | async-start | bytes 2359296 | tf_op jit(solution)/shard_map/all_gather | solution.py:102
  74.0 99.2 %copy-start.51 = (s32[2,56]{1,0:T(2,128)S(1)}, s32[2,56]{1,0:T(2,128)}, u32[]{:S(2)}) copy-start(s32[2,56]{1,0:T(2,128)} %param.9) | copy-start | bytes 1348
  173.1 234.0 %all-gather.9.cloned.1.call-start = ((), (), s32[]{:S(2)}) async-start(), calls=%async_computation.4 | async-start | bytes 7798784 | tf_op jit(solution)/shard_map/all_gather | solution.py:100
  175.0 305.8 %all-to-all-start.2 = ((s32[16,1,1]{2,1,0:T(1,128)}), s32[16,1,1]{2,1,0:T(1,128)S(1)}, u32[]{:S(2)}, u32[]{:S(2)}) async-start(s32[16,1,1]{2,1,0:T(1,128)} %copy.140), calls=%async_computation.2 | async-start | bytes 16384 | tf_op jit(solution)/shard_map/all_to_all | solution.py:169
  301.2 98.7 %copy-start.1 = (f32[896,128]{1,0:T(8,128)S(1)}, f32[896,128]{1,0:T(8,128)}, u32[]{:S(2)}) copy-start(f32[896,128]{1,0:T(8,128)} %copy-done) | copy-start | bytes 1376260
  313.9 86.9 %copy-start.3 = (f32[768,128]{1,0:T(8,128)S(1)}, f32[768,128]{1,0:T(8,128)}, u32[]{:S(2)}) copy-start(f32[768,128]{1,0:T(8,128)} %copy-done.2) | copy-start | bytes 1179652
  325.3 76.4 %copy-start.18 = (f32[128,128]{1,0:T(8,128)}, f32[128,128]{1,0:T(8,128)S(1)}, u32[]{:S(2)}) copy-start(f32[128,128]{1,0:T(8,128)S(1)} %fusion.37) | copy-start | bytes 196612
  325.8 76.3 %copy-start.7 = (f32[384,128]{1,0:T(8,128)}, f32[384,128]{1,0:T(8,128)S(1)}, u32[]{:S(2)}) copy-start(f32[384,128]{1,0:T(8,128)S(1)} %fusion.47) | copy-start | bytes 589828
  326.5 22.9 %copy-start.11 = (f32[384,384]{0,1:T(8,128)}, f32[384,384]{0,1:T(8,128)S(1)}, u32[]{:S(2)}) copy-start(f32[384,384]{0,1:T(8,128)S(1)} %convolution_subtract_fusion.6) | copy-start | bytes 1769476
  326.5 75.2 %copy-start.32 = (f32[128,128]{1,0:T(8,128)S(1)}, f32[128,128]{1,0:T(8,128)}, u32[]{:S(2)}) copy-start(f32[128,128]{1,0:T(8,128)} %get-tuple-element.31) | copy-start | bytes 196612
  326.5 75.2 %copy-start.36 = (f32[1024]{0:T(1024)S(1)}, f32[1024]{0:T(1024)}, u32[]{:S(2)}) copy-start(f32[1024]{0:T(1024)} %pad.10.clone) | copy-start | bytes 12292
  326.5 75.4 %copy-start.35 = (f32[128,128]{1,0:T(8,128)S(1)}, f32[128,128]{1,0:T(8,128)}, u32[]{:S(2)}) copy-start(f32[128,128]{1,0:T(8,128)} %get-tuple-element.29) | copy-start | bytes 196612
  326.5 75.4 %copy-start.38 = (f32[1024]{0:T(1024)S(1)}, f32[1024]{0:T(1024)}, u32[]{:S(2)}) copy-start(f32[1024]{0:T(1024)} %pad.13.clone) | copy-start | bytes 12292
  338.4 63.8 %copy-start.33 = (f32[128,128]{1,0:T(8,128)S(1)}, f32[128,128]{1,0:T(8,128)}, u32[]{:S(2)}) copy-start(f32[128,128]{1,0:T(8,128)} %get-tuple-element.27) | copy-start | bytes 196612
  338.4 63.8 %copy-start.37 = (f32[1024]{0:T(1024)S(1)}, f32[1024]{0:T(1024)}, u32[]{:S(2)}) copy-start(f32[1024]{0:T(1024)} %pad.16.clone) | copy-start | bytes 12292
  350.1 52.3 %copy-start.20 = (f32[128,128]{1,0:T(8,128)}, f32[128,128]{1,0:T(8,128)S(1)}, u32[]{:S(2)}) copy-start(f32[128,128]{1,0:T(8,128)S(1)} %fusion.35) | copy-start | bytes 196612
  351.5 51.0 %copy-start.9 = (f32[256,128]{1,0:T(8,128)}, f32[256,128]{1,0:T(8,128)S(1)}, u32[]{:S(2)}) copy-start(f32[256,128]{1,0:T(8,128)S(1)} %fusion.49) | copy-start | bytes 393220
  376.1 26.8 %copy-start.24 = (f32[128,128]{1,0:T(8,128)}, f32[128,128]{1,0:T(8,128)S(1)}, u32[]{:S(2)}) copy-start(f32[128,128]{1,0:T(8,128)S(1)} %fusion.33) | copy-start | bytes 196612
  376.4 26.5 %copy-start.12 = (f32[128,128]{1,0:T(8,128)}, f32[128,128]{1,0:T(8,128)S(1)}, u32[]{:S(2)}) copy-start(f32[128,128]{1,0:T(8,128)S(1)} %fusion.51) | copy-start | bytes 196612
  376.7 26.2 %copy-start.49 = (s32[128]{0:T(128)S(1)}, s32[128]{0:T(128)}, u32[]{:S(2)}) copy-start(s32[128]{0:T(128)} %get-tuple-element.56) | copy-start | bytes 1540
  376.7 26.2 %copy-start.50 = (s32[128]{0:T(128)S(1)}, s32[128]{0:T(128)}, u32[]{:S(2)}) copy-start(s32[128]{0:T(128)} %get-tuple-element.57) | copy-start | bytes 1540
  376.8 27.1 %copy-start.43 = (pred[4]{0:T(512)(128)(4,1)S(1)}, pred[4]{0:T(512)(128)(4,1)}, u32[]{:S(2)}) copy-start(pred[4]{0:T(512)(128)(4,1)} %get-tuple-element.55) | copy-start | bytes 16
  464.4 6.3 %copy-start.15 = (f32[128,4,128]{2,1,0:T(4,128)S(1)}, f32[128,4,128]{2,1,0:T(4,128)}, u32[]{:S(2)}) copy-start(f32[128,4,128]{2,1,0:T(4,128)} %broadcast_select_fusion) | copy-start | bytes 786436
  464.4 6.3 %copy-start.40 = (s32[8]{0:T(128)S(1)}, s32[8]{0:T(128)}, u32[]{:S(2)}) copy-start(s32[8]{0:T(128)} %copy-done.39) | copy-start | bytes 100
  464.4 6.3 %copy-start.42 = (pred[8]{0:T(512)(128)(4,1)S(1)}, pred[8]{0:T(512)(128)(4,1)}, u32[]{:S(2)}) copy-start(pred[8]{0:T(512)(128)(4,1)} %copy-done.41) | copy-start | bytes 28
  464.5 6.3 %copy-start.46 = (pred[8]{0:T(512)(128)(4,1)S(1)}, pred[8]{0:T(512)(128)(4,1)}, u32[]{:S(2)}) copy-start(pred[8]{0:T(512)(128)(4,1)} %copy-done.45) | copy-start | bytes 28
  480.9 7.7 %copy-start.52 = (s32[2,56]{1,0:T(2,128)S(1)}, s32[2,56]{1,0:T(2,128)}, u32[]{:S(2)}) copy-start(s32[2,56]{1,0:T(2,128)} %param.9) | copy-start | bytes 1348
  480.9 8.4 %copy-start.23 = (f32[128,128]{1,0:T(8,128)S(1)}, f32[128,128]{1,0:T(8,128)}, u32[]{:S(2)}) copy-start(f32[128,128]{1,0:T(8,128)} %copy-done.22) | copy-start | bytes 196612
  480.9 100.3 %all-to-all-start.1 = ((f32[16,1,65536]{2,1,0:T(1,128)}), f32[16,1,65536]{2,1,0:T(1,128)}, u32[]{:S(2)}, u32[]{:S(2)}) async-start(f32[16,1,65536]{2,1,0:T(1,128)} %copy.139), calls=%async_computation.1 | async-start | bytes 8388608 | tf_op jit(solution)/shard_map/all_to_all | solution.py:168
  (29 other events, 70.8 us)
Sparse Core Ops, SparseCore 0:
  11.0 50.0 all-gather.6
  173.2 32.6 all-gather.10
  208.4 73.2 all-gather.8
